TPU v7x, 32 devices: a whole 2x2x4 slice. The times are simulated.
32 devices in a mesh: clips: 2 (over y), frame: 4 (over x, core), row: 4 (over z).
Axes of the slice: x: 2, y: 2, z: 4, core: 2. Of those that a mesh axis runs over, the one named last changes fastest.
Arguments:
- frames: bfloat16 [16, 512, 640], P(('clips', 'frame'), 'row'), parts along dimension 0, may hold values from -16 to 16
- key_index: int32 [4], P('clips'), parts along dimension 0, may hold values from 0 to 7, as said below
- w_query: bfloat16 [640, 640], replicated, may hold values from -0.25 to 0.25
- w_keyval: bfloat16 [640, 1280], replicated, may hold values from -0.25 to 0.25
- w_out: bfloat16 [640, 640], replicated, may hold values from -0.25 to 0.25
- norm_gain: float32 [640], replicated, may hold values from 0.1 to 1.9
- w_first: bfloat16 [3, 640, 640], replicated, may hold values from -0.125 to 0.125
- w_second: bfloat16 [3, 640, 640], replicated, may hold values from -0.125 to 0.125
Outputs:
- edited: bfloat16 [16, 512, 640], P(('clips', 'frame'), 'row'), parts along dimension 0
There are 2 independent parts, one for each index of `clips`. A program takes and returns all parts, laid end to end along the dimension named above; an argument that names none is the same for every part. Nothing has to cross between parts.
Inputs may be any that keep to these rules, and one draw needn't show every extreme that they name: `key_index`: two different frame indices of the window, in either order; one of them is the window's last frame 8 - 1.
All inputs are finite; a program needn't handle non-finite values.
Results may differ from a plain program's by a relative error of at most 0.0067.
Values may be sent and summed in bfloat16 or wider, within the bound.
No kernel may reach another device: no remote copies, remote signals or barrier semaphores. Data moves between devices by JAX's collectives and lax.ppermute only.
A program may use at most 128 MiB of HBM per device.

v0:
```python
from functools import partial
import jax
import jax.numpy as jnp
from jax import lax
from jax.sharding import PartitionSpec as P

HEADS = 10
HEAD_DIM = 64


def from_root(value, axis, source):
    kept = jnp.where(lax.axis_index(axis) == source, value, 0).astype(value.dtype)
    return lax.psum(kept, axis)


def extended(array, sides, width):
    for axis, dim in sides:
        size, length = (lax.axis_size(axis), array.shape[dim])
        up = [(i, (i + 1) % size) for i in range(size - 1)]
        down = [(j, i) for i, j in up]
        last = lax.slice_in_dim(array, length - width, length, axis=dim)
        first = lax.slice_in_dim(array, 0, width, axis=dim)
        before = lax.ppermute(last, axis, up)
        after = lax.ppermute(first, axis, down)
        array = jnp.concatenate([before, array, after], axis=dim)
    return array


def temporal_mix(padded, weights, count):
    result = jnp.zeros((count * padded.shape[1], padded.shape[2]), jnp.float32)
    for offset in range(3):
        window = padded[offset : offset + count].reshape(-1, padded.shape[2])
        result = result + jnp.dot(window, weights[offset], preferred_element_type=jnp.float32)
    return result


def absorb_keys(query_heads, channels, state_now, kv_pieces, piece_start):
    highest, denominator, accumulated = state_now
    joined = jnp.concatenate(kv_pieces, axis=0)
    key_heads = joined[:, :channels].reshape(-1, HEADS, HEAD_DIM)
    value_heads = joined[:, channels:].reshape(-1, HEADS, HEAD_DIM)
    scores = jnp.einsum(
        "qhd,khd->hqk", query_heads, key_heads, preferred_element_type=jnp.float32
    ) * HEAD_DIM ** (-0.5)
    raised = jnp.maximum(highest, jnp.max(scores, axis=-1))
    kept_frac = jnp.exp(highest - raised)
    exponent = jnp.exp(scores - raised[:, :, None])
    denominator = jnp.sum(exponent, axis=-1)
    contrib = jnp.einsum(
        "hqk,khd->qhd",
        exponent.astype(jnp.bfloat16),
        value_heads,
        preferred_element_type=jnp.float32,
    )
    accumulated = accumulated * jnp.repeat(kept_frac.T, HEAD_DIM, axis=1) + contrib.reshape(
        contrib.shape[0], -1
    )
    return (raised, denominator, accumulated)


def shards(frames, key_index, w_query, w_keyval, w_out, norm_gain, w_first, w_second):
    frame_count, row_count, channels = frames.shape
    flattened = frames.reshape(-1, channels)
    queries = jnp.dot(flattened, w_query, preferred_element_type=jnp.float32).astype(jnp.bfloat16)
    query_heads = queries.reshape(-1, HEADS, HEAD_DIM)
    query_total = queries.shape[0]
    owners = key_index // frame_count
    chosen = frames[key_index % frame_count].reshape(-1, channels)
    keyval = jnp.dot(chosen, w_keyval, preferred_element_type=jnp.float32).astype(jnp.bfloat16)
    own_parts = (keyval[:row_count], keyval[row_count:])
    initial = (
        jnp.full((HEADS, query_total), -1e30, jnp.float32),
        jnp.zeros((HEADS, query_total), jnp.float32),
        jnp.zeros((query_total, channels), jnp.float32),
    )
    absorb = partial(absorb_keys, query_heads, channels)
    spread_parts = []
    for key_slot in range(2):
        spread_parts.append(from_root(own_parts[key_slot], "frame", owners[key_slot]))
    final = absorb(
        initial,
        (
            lax.all_gather(spread_parts[0], "row", axis=0, tiled=True),
            lax.all_gather(spread_parts[1], "row", axis=0, tiled=True),
        ),
        jnp.int32(0),
    )
    highest, denominator, accumulated = final
    mixed = accumulated.reshape(query_total, HEADS, HEAD_DIM) / denominator.T[:, :, None]
    attended = mixed.reshape(query_total, channels).astype(jnp.bfloat16)
    residual = flattened.astype(jnp.float32) + jnp.dot(
        attended, w_out, preferred_element_type=jnp.float32
    )
    mean_square = jnp.mean(residual * residual, axis=-1, keepdims=True)
    normed = (residual * lax.rsqrt(mean_square + 1e-06) * norm_gain).astype(jnp.bfloat16)
    normed = normed.reshape(frame_count, row_count, channels)
    padded = extended(normed, (("frame", 0),), 1)
    hidden = jax.nn.silu(temporal_mix(padded, w_first, frame_count)).astype(jnp.bfloat16)
    hidden = hidden.reshape(frame_count, row_count, channels)
    padded = extended(hidden, (("frame", 0),), 1)
    second = temporal_mix(padded, w_second, frame_count)
    return (residual + second).astype(jnp.bfloat16).reshape(frame_count, row_count, channels)


def solution(mesh):
    return jax.shard_map(
        shards,
        mesh=mesh,
        in_specs=(P(("clips", "frame"), "row", None), P("clips"), P(), P(), P(), P(), P(), P()),
        out_specs=P(("clips", "frame"), "row", None),
        check_vma=False,
    )
```

profile of v0, /device:TPU:1, one launch (start us, length us, event | category | flops | bytes accessed | tf_op | source)
XLA Modules:
  0.0 162.4 jit_solution(13678371207064377667)
XLA Ops:
  6.5 0.0 copy-start
  6.5 0.0 all-reduce.3.cloned.1.call-start
  6.5 0.8 and_select_fusion.1
  7.3 0.6 fusion.42
  9.2 1.6 gather_fusion
  10.8 0.0 copy-done
  10.8 0.0 copy-start.1
  10.8 0.0 copy-start.5
  10.8 0.7 convolution_convert_fusion
  11.5 0.9 slice_select_fusion
  12.4 0.0 all-reduce.3.cloned.1.call-update
  12.5 0.0 all-gather.3.cloned.1.call-start
  12.5 34.7 %all-reduce.3.cloned.1.call-done = (bf16[128,1280]{1,0:T(8,128)(2,1)}, bf16[128,1280]{1,0:T(8,128)(2,1)}) async-done(((bf16[128,1280]{1,0:T(8,128)(2,1)}, bf16[128,1280]{1,0:T(8,128)(2,1)}), (bf16[128,1280]{1,0:T(8,128)(2,1)}, bf16[128,1280]{1,0:T(8,128)(2,1)})) %all-reduce.3.cloned.1.call-update) | async-done | bytes 655376 | tf_op jit(solution)/shard_map/psum | solution.py:13
  47.2 0.0 all-gather.3.cloned.1.call-update
  47.2 0.0 all-gather.5.cloned.1.call-start
  47.3 0.7 all-gather.5.cloned.1.call-update
  48.0 0.0 copy-done.1
  48.0 0.0 copy-done.5
  48.0 0.5 convolution_convert_fusion.1
  48.4 0.9 copy.12
  49.4 32.9 %all-gather.3.cloned.1.call-done = bf16[512,1280]{1,0:T(8,128)(2,1)} async-done(((bf16[128,1280]{1,0:T(8,128)(2,1)}), bf16[512,1280]{1,0:T(8,128)(2,1)}) %all-gather.3.cloned.1.call-update) | async-done | bytes 1310736 | tf_op jit(solution)/shard_map/all_gather | solution.py:83
  82.2 2.5 %constant_dynamic-update-slice_fusion.1 = bf16[1024,1280]{1,0:T(8,128)(2,1)} fusion(bf16[512,1280]{1,0:T(8,128)(2,1)} %all-gather.3.cloned.1.call-done), kind=kLoop, calls=%fused_computation.54 | loop fusion | bytes 2621440
  84.7 30.8 %all-gather.5.cloned.1.call-done = bf16[512,1280]{1,0:T(8,128)(2,1)} async-done(((bf16[128,1280]{1,0:T(8,128)(2,1)}), bf16[512,1280]{1,0:T(8,128)(2,1)}) %all-gather.5.cloned.1.call-update) | async-done | bytes 1310736 | tf_op jit(solution)/shard_map/all_gather | solution.py:84
  115.5 2.5 %constant_dynamic-update-slice_fusion = bf16[1024,1280]{1,0:T(8,128)(2,1)} fusion(bf16[1024,1280]{1,0:T(8,128)(2,1)} %constant_dynamic-update-slice_fusion.1, bf16[512,1280]{1,0:T(8,128)(2,1)} %all-gather.5.cloned.1.call-done), kind=kLoop, calls=%fused_computation.53 | loop fusion | bytes 2621440 | tf_op jit(solution)/shard_map/concatenate | solution.py:39
  118.0 3.5 %fusion.41 = (bf16[1024,640]{1,0:T(8,128)(2,1)}, bf16[1024,640]{1,0:T(8,128)(2,1)}) fusion(bf16[1024,1280]{1,0:T(8,128)(2,1)} %constant_dynamic-update-slice_fusion), kind=kLoop, calls=%fused_computation.63 | loop fusion | bytes 5242880 | tf_op jit(solution)/shard_map/slice | solution.py:40
  121.5 1.6 copy.13
  123.1 2.5 %copy.14 = bf16[1024,640]{0,1:T(8,128)(2,1)} copy(bf16[1024,640]{1,0:T(8,128)(2,1)} %get-tuple-element.8) | data formatting | bytes 2621440 | tf_op jit(solution)/shard_map/slice | solution.py:41
  125.5 2.6 %multiply_reduce_fusion = (f32[10,256]{1,0:T(8,128)S(1)}, f32[10,256,1024]{2,1,0:T(8,128)S(1)}) fusion(bf16[256,10,64]{0,2,1:T(8,128)(2,1)} %bitcast.74, bf16[1024,10,64]{0,2,1:T(8,128)(2,1)S(1)} %bitcast.69), kind=kOutput, calls=%fused_computation.2 | convolution fusion | flops 340784640 | bytes 12134400 | tf_op jit(solution)/shard_map/qhd,khd->hqk/dot_general | solution.py:42
  128.2 0.0 copy-start.3
  128.2 2.1 %fusion = f32[10,256]{1,0:T(8,128)S(1)} fusion(f32[10,256,1024]{2,1,0:T(8,128)S(1)} %get-tuple-element.26, f32[10,256]{1,0:T(8,128)S(1)} %get-tuple-element.20), kind=kLoop, calls=%fused_computation.3 | loop fusion | flops 7861760 | bytes 10506240 | tf_op jit(solution)/shard_map/reduce_sum | solution.py:48
  130.2 0.0 copy-done.3
  130.2 0.0 copy-start.6
  130.3 0.0 copy-start.7
  130.3 2.3 %fusion.19 = bf16[256,10,64]{0,2,1:T(8,128)(2,1)S(1)} fusion(bf16[1024,10,64]{0,2,1:T(8,128)(2,1)S(1)} %bitcast.77, f32[10,256,1024]{2,1,0:T(8,128)S(1)} %get-tuple-element.26, f32[10,256]{1,0:T(8,128)S(1)} %get-tuple-element.20, f32[256,10]{0,1:T(8,128)S(1)} %bitcast.82, f32[256,10]{0,1:T(8,128)S(1)} %get-tuple-element.19), kind=kOutput, calls=%fused_computation.20 | convolution fusion | flops 343900160 | bytes 12154880 | tf_op jit(solution)/shard_map/hqk,khd->qhd/dot_general | solution.py:49
  132.6 0.0 copy-start.4
  132.6 0.0 copy-done.6
  132.6 0.6 multiply_reduce_fusion.1
  133.2 0.0 copy-done.7
  133.2 0.1 multiply_convert_fusion.1
  133.4 4.3 %collective-permute-start = (bf16[1,128,640]{2,1,0:T(8,128)(2,1)S(1)}, bf16[1,128,640]{2,1,0:T(8,128)(2,1)S(1)}, u32[]{:S(2)}, u32[]{:S(2)}) collective-permute-start(bf16[1,128,640]{2,1,0:T(8,128)(2,1)S(1)} %get-tuple-element.17), channel_id=1, source_target_pairs={{0,4},{4,8},{8,12},{1,5},{5,9},{9,13},{2,6},{6,10},{10,14},{3,7},{... | collective-permute-start | bytes 491528 | tf_op jit(solution)/shard_map/ppermute | solution.py:23
  137.7 1.9 %collective-permute-start.1 = (bf16[1,128,640]{2,1,0:T(8,128)(2,1)S(1)}, bf16[1,128,640]{2,1,0:T(8,128)(2,1)S(1)}, u32[]{:S(2)}, u32[]{:S(2)}) collective-permute-start(bf16[1,128,640]{2,1,0:T(8,128)(2,1)S(1)} %get-tuple-element.18), channel_id=1, source_target_pairs={{4,0},{8,4},{12,8},{5,1},{9,5},{13,9},{6,2},{10,6},{14,10},{7,3},{... | collective-permute-start | bytes 491528 | tf_op jit(solution)/shard_map/ppermute | solution.py:24
  139.6 0.0 copy-done.4
  139.6 0.5 fusion.29
  140.1 0.0 collective-permute-done
  140.1 4.2 %collective-permute-done.1 = bf16[1,128,640]{2,1,0:T(8,128)(2,1)S(1)} collective-permute-done((bf16[1,128,640]{2,1,0:T(8,128)(2,1)S(1)}, bf16[1,128,640]{2,1,0:T(8,128)(2,1)S(1)}, u32[]{:S(2)}, u32[]{:S(2)}) %collective-permute-start.1) | collective-permute-done | bytes 163872 | tf_op jit(solution)/shard_map/ppermute | solution.py:24
  144.3 0.1 pad_maximum_fusion.3
  144.4 0.5 fusion.27
  144.9 0.0 copy-start.2
  144.9 0.5 multiply_convert_fusion
  145.4 2.1 %collective-permute-start.2 = (bf16[1,128,640]{2,1,0:T(8,128)(2,1)S(1)}, bf16[1,128,640]{2,1,0:T(8,128)(2,1)S(1)}, u32[]{:S(2)}, u32[]{:S(2)}) collective-permute-start(bf16[1,128,640]{2,1,0:T(8,128)(2,1)S(1)} %get-tuple-element.13), channel_id=1, source_target_pairs={{0,4},{4,8},{8,12},{1,5},{5,9},{9,13},{2,6},{6,10},{10,14},{3,7},{... | collective-permute-start | bytes 491528 | tf_op jit(solution)/shard_map/ppermute | solution.py:23
  147.5 2.4 %collective-permute-start.3 = (bf16[1,128,640]{2,1,0:T(8,128)(2,1)S(1)}, bf16[1,128,640]{2,1,0:T(8,128)(2,1)S(1)}, u32[]{:S(2)}, u32[]{:S(2)}) collective-permute-start(bf16[1,128,640]{2,1,0:T(8,128)(2,1)S(1)} %get-tuple-element.14), channel_id=1, source_target_pairs={{4,0},{8,4},{12,8},{5,1},{9,5},{13,9},{6,2},{10,6},{14,10},{7,3},{... | collective-permute-start | bytes 491528 | tf_op jit(solution)/shard_map/ppermute | solution.py:24
  149.9 0.0 copy-done.2
  149.9 0.5 fusion.24
  150.4 0.0 collective-permute-done.2
  150.4 3.7 %collective-permute-done.3 = bf16[1,128,640]{2,1,0:T(8,128)(2,1)S(1)} collective-permute-done((bf16[1,128,640]{2,1,0:T(8,128)(2,1)S(1)}, bf16[1,128,640]{2,1,0:T(8,128)(2,1)S(1)}, u32[]{:S(2)}, u32[]{:S(2)}) %collective-permute-start.3) | collective-permute-done | bytes 163872 | tf_op jit(solution)/shard_map/ppermute | solution.py:24
  154.1 0.1 pad_maximum_fusion.1
  154.2 0.5 fusion.22
  154.7 1.2 fusion.15
  (5 shorter events, 0.1 us)
Async XLA Ops:
  6.5 4.3 %copy-start = (bf16[640,1280]{1,0:T(8,128)(2,1)S(1)}, bf16[640,1280]{1,0:T(8,128)(2,1)}, u32[]{:S(2)}) copy-start(bf16[640,1280]{1,0:T(8,128)(2,1)} %param.11) | copy-start | bytes 4915204
  6.5 40.7 %all-reduce.3.cloned.1.call-start = ((), (), s32[]{:S(2)}) async-start(), calls=%async_computation.2 | async-start | bytes 1310720 | tf_op jit(solution)/shard_map/psum | solution.py:13
  10.8 37.2 %copy-start.1 = (bf16[2,128,640]{2,1,0:T(8,128)(2,1)S(1)}, bf16[2,128,640]{2,1,0:T(8,128)(2,1)}, u32[]{:S(2)}) copy-start(bf16[2,128,640]{2,1,0:T(8,128)(2,1)} %param.8) | copy-start | bytes 983044
  10.8 37.2 %copy-start.5 = (bf16[640,640]{1,0:T(8,128)(2,1)S(1)}, bf16[640,640]{1,0:T(8,128)(2,1)}, u32[]{:S(2)}) copy-start(bf16[640,640]{1,0:T(8,128)(2,1)} %param.10) | copy-start | bytes 2457604
  12.5 69.8 %all-gather.3.cloned.1.call-start = ((), (), s32[]{:S(2)}) async-start(), calls=%async_computation | async-start | bytes 1638400 | tf_op jit(solution)/shard_map/all_gather | solution.py:83
  47.2 68.3 %all-gather.5.cloned.1.call-start = ((), (), s32[]{:S(2)}) async-start(), calls=%async_computation.1 | async-start | bytes 1638400 | tf_op jit(solution)/shard_map/all_gather | solution.py:84
  128.2 2.1 %copy-start.3 = (bf16[1024,640]{0,1:T(8,128)(2,1)S(1)}, bf16[1024,640]{0,1:T(8,128)(2,1)}, u32[]{:S(2)}) copy-start(bf16[1024,640]{0,1:T(8,128)(2,1)} %copy.14) | copy-start | bytes 3932164
  130.2 2.3 %copy-start.6 = (bf16[640,640]{1,0:T(8,128)(2,1)S(1)}, bf16[640,640]{1,0:T(8,128)(2,1)}, u32[]{:S(2)}) copy-start(bf16[640,640]{1,0:T(8,128)(2,1)} %param.12) | copy-start | bytes 2457604
  130.3 2.9 %copy-start.7 = (f32[640]{0:T(1024)S(1)}, f32[640]{0:T(1024)}, u32[]{:S(2)}) copy-start(f32[640]{0:T(1024)} %param.13) | copy-start | bytes 7684
  132.6 7.1 %copy-start.4 = (bf16[3,640,640]{2,1,0:T(8,128)(2,1)S(1)}, bf16[3,640,640]{2,1,0:T(8,128)(2,1)}, u32[]{:S(2)}) copy-start(bf16[3,640,640]{2,1,0:T(8,128)(2,1)} %param.14) | copy-start | bytes 7372804
  133.4 6.7 %collective-permute-start = (bf16[1,128,640]{2,1,0:T(8,128)(2,1)S(1)}, bf16[1,128,640]{2,1,0:T(8,128)(2,1)S(1)}, u32[]{:S(2)}, u32[]{:S(2)}) collective-permute-start(bf16[1,128,640]{2,1,0:T(8,128)(2,1)S(1)} %get-tuple-element.17), channel_id=1, source_target_pairs={{0,4},{4,8},{8,12},{1,5},{5,9},{9,13},{2,6},{6,10},{10,14},{3,7},{... | collective-permute-start | bytes 491528 | tf_op jit(solution)/shard_map/ppermute | solution.py:23
  137.7 6.6 %collective-permute-start.1 = (bf16[1,128,640]{2,1,0:T(8,128)(2,1)S(1)}, bf16[1,128,640]{2,1,0:T(8,128)(2,1)S(1)}, u32[]{:S(2)}, u32[]{:S(2)}) collective-permute-start(bf16[1,128,640]{2,1,0:T(8,128)(2,1)S(1)} %get-tuple-element.18), channel_id=1, source_target_pairs={{4,0},{8,4},{12,8},{5,1},{9,5},{13,9},{6,2},{10,6},{14,10},{7,3},{... | collective-permute-start | bytes 491528 | tf_op jit(solution)/shard_map/ppermute | solution.py:24
  144.9 5.1 %copy-start.2 = (bf16[3,640,640]{2,1,0:T(8,128)(2,1)S(1)}, bf16[3,640,640]{2,1,0:T(8,128)(2,1)}, u32[]{:S(2)}) copy-start(bf16[3,640,640]{2,1,0:T(8,128)(2,1)} %param.15) | copy-start | bytes 7372804
  145.4 5.0 %collective-permute-start.2 = (bf16[1,128,640]{2,1,0:T(8,128)(2,1)S(1)}, bf16[1,128,640]{2,1,0:T(8,128)(2,1)S(1)}, u32[]{:S(2)}, u32[]{:S(2)}) collective-permute-start(bf16[1,128,640]{2,1,0:T(8,128)(2,1)S(1)} %get-tuple-element.13), channel_id=1, source_target_pairs={{0,4},{4,8},{8,12},{1,5},{5,9},{9,13},{2,6},{6,10},{10,14},{3,7},{... | collective-permute-start | bytes 491528 | tf_op jit(solution)/shard_map/ppermute | solution.py:23
  147.5 6.6 %collective-permute-start.3 = (bf16[1,128,640]{2,1,0:T(8,128)(2,1)S(1)}, bf16[1,128,640]{2,1,0:T(8,128)(2,1)S(1)}, u32[]{:S(2)}, u32[]{:S(2)}) collective-permute-start(bf16[1,128,640]{2,1,0:T(8,128)(2,1)S(1)} %get-tuple-element.14), channel_id=1, source_target_pairs={{4,0},{8,4},{12,8},{5,1},{9,5},{13,9},{6,2},{10,6},{14,10},{7,3},{... | collective-permute-start | bytes 491528 | tf_op jit(solution)/shard_map/ppermute | solution.py:24
Sparse Core Ops, SparseCore 0:
  12.6 34.5 all-reduce.2
  48.8 33.4 all-gather.2
  83.8 31.6 all-gather.4
where the time goes:
time: 163 us; the launch traced here: 162 us
  waiting for transfers between devices  107 us (66%)
  local copies, waits for them, and re-layouts  15.6 us (10%)
  between operations  14.7 us (9%)
  starting transfers between devices  10.8 us (7%)
  matrix products  10.2 us (6%)
  other arithmetic  4.05 us (2%)
    psum x1, waiting for transfers between devices, from_root(): return lax.psum(kept, axis)  34.7 us
    all_gather x1, waiting for transfers between devices, shards(): lax.all_gather(spread_parts[0], 'row', axis=0, tiled=True)  32.9 us
    all_gather x1, waiting for transfers between devices, shards(): lax.all_gather(spread_parts[1], 'row', axis=0, tiled=True)  30.8 us
    ppermute x2, waiting for transfers between devices, extended(): after = lax.ppermute(first, axis, down)  7.96 us
    ppermute x2, starting transfers between devices, extended(): before = lax.ppermute(last, axis, up)  6.37 us
    slice x2, local copies, waits for them, and re-layouts, absorb_keys(): key_heads = joined[:, :channels].reshape(-1, HEADS, HEAD_DIM)  5.06 us
    ppermute x2, starting transfers between devices, extended(): after = lax.ppermute(first, axis, down)  4.33 us
    dot_general x6, matrix products, temporal_mix(): jnp.dot(window, weights[offset], preferred_element_type=jnp.float32)  3.53 us
  transfers between devices with their start and end apart: 7, of which 5 were waited for; matrix products, arithmetic and copies ran while one was open for 3% of the time, Pallas kernels for 0%

commit v1 on v0

--- a/solution.py
+++ b/solution.py
@@ -6,6 +6,28 @@
 
 HEADS = 10
 HEAD_DIM = 64
+
+
+def joined_along(parts, dim):
+    shape = list(parts.shape[1:])
+    shape[dim] *= parts.shape[0]
+    return jnp.moveaxis(parts, 0, dim).reshape(shape)
+
+
+def grow_blocks(array, axis):
+    devices = lax.axis_size(axis)
+    tiles = array[None]
+    for level in range(devices.bit_length() - 1):
+        bit = 1 << level
+        theirs = lax.ppermute(tiles, axis, [(i, i ^ bit) for i in range(devices)])
+        both = jnp.stack([tiles, theirs])
+        upper = lax.axis_index(axis) >> level & 1
+        tiles = jnp.where(upper == 0, both, both[::-1]).reshape(-1, *array.shape)
+    return tiles
+
+
+def collect(x, axis, dim):
+    return joined_along(grow_blocks(x, axis), dim)
 
 
 def from_root(value, axis, source):
@@ -80,7 +102,7 @@
     final = absorb(
         initial,
         (
-            lax.all_gather(spread_parts[0], "row", axis=0, tiled=True),
+            collect(spread_parts[0], "row", 0),
             lax.all_gather(spread_parts[1], "row", axis=0, tiled=True),
         ),
         jnp.int32(0),

time: 163 us -> 156 us (0.957)
  waiting for transfers between devices: 107 us -> 96.2 us
  local copies, waits for them, and re-layouts: 15.6 us -> 7.25 us
  other arithmetic: 4.05 us -> 10.4 us
  starting transfers between devices: 10.8 us -> 15.1 us
    ppermute x0 -> x2, waiting for transfers between devices: none -> 53.5 us  [grow_blocks(): theirs = lax.ppermute(tiles, axis, [(i, i ^ bit) for i in range(devices)])]
    all_gather x1 -> x0, waiting for transfers between devices: 32.9 us -> none  [shards(): lax.all_gather(spread_parts[0], 'row', axis=0, tiled=True)]
    all_gather x1, waiting for transfers between devices: 30.8 us -> 0.02 us  [shards(): lax.all_gather(spread_parts[1], 'row', axis=0, tiled=True)]
    ppermute x0 -> x2, starting transfers between devices: none -> 4.33 us  [grow_blocks(): theirs = lax.ppermute(tiles, axis, [(i, i ^ bit) for i in range(devices)])]
    slice x2 -> x1, local copies, waits for them, and re-layouts: 5.06 us -> 1.6 us  [absorb_keys(): key_heads = joined[:, :channels].reshape(-1, HEADS, HEAD_DIM)]
    another operation x0 -> x3, other arithmetic: none -> 3.2 us  [grow_blocks(): both = jnp.stack([tiles, theirs])]
    concatenate x0 -> x1, other arithmetic: none -> 2.97 us  [absorb_keys(): joined = jnp.concatenate(kv_pieces, axis=0)]
    unnamed x17 -> x14, local copies, waits for them, and re-layouts: 2.52 us -> 0.04 us
  transfers between devices with their start and end apart: 7 -> 8, of which waited for: 5 -> 5; matrix products, arithmetic and copies ran while one was open for 3% -> 4% of each run, Pallas kernels for 0% -> 0%
where the time goes in v1:
time: 156 us; the launch traced here: 155 us
  waiting for transfers between devices  96.2 us (62%)
  starting transfers between devices  15.1 us (10%)
  between operations  15 us (10%)
  matrix products  11.3 us (7%)
  other arithmetic  10.4 us (7%)
  local copies, waits for them, and re-layouts  7.25 us (5%)
    ppermute x2, waiting for transfers between devices, grow_blocks(): theirs = lax.ppermute(tiles, axis, [(i, i ^ bit) for i in range(devices)])  53.5 us
    psum x1, waiting for transfers between devices, from_root(): return lax.psum(kept, axis)  34.7 us
    ppermute x2, waiting for transfers between devices, extended(): after = lax.ppermute(first, axis, down)  7.96 us
    ppermute x2, starting transfers between devices, extended(): before = lax.ppermute(last, axis, up)  6.41 us
    ppermute x2, starting transfers between devices, grow_blocks(): theirs = lax.ppermute(tiles, axis, [(i, i ^ bit) for i in range(devices)])  4.33 us
    ppermute x2, starting transfers between devices, extended(): after = lax.ppermute(first, axis, down)  4.33 us
    dot_general x6, matrix products, temporal_mix(): jnp.dot(window, weights[offset], preferred_element_type=jnp.float32)  3.53 us
    another operation x3, other arithmetic, grow_blocks(): both = jnp.stack([tiles, theirs])  3.2 us
  transfers between devices with their start and end apart: 8, of which 5 were waited for; matrix products, arithmetic and copies ran while one was open for 4% of the time, Pallas kernels for 0%

profile of v1, /device:TPU:1, one launch (start us, length us, event | category | flops | bytes accessed | tf_op | source)
XLA Modules:
  0.0 155.3 jit_solution(17334580482452409395)
XLA Ops:
  6.5 0.0 copy-start
  6.5 0.0 all-reduce.3.cloned.1.call-start
  6.5 0.8 and_select_fusion.1
  7.3 0.6 fusion.44
  9.2 1.6 %gather_fusion = bf16[2,128,640]{2,1,0:T(8,128)(2,1)S(1)} fusion(bf16[2,128,640]{2,1,0:T(8,128)(2,1)} %param.8, s32[1024]{0:T(1024)S(1)} %pad_clamp_fusion), kind=kCustom, calls=%fused_computation | custom fusion | bytes 655368 | tf_op jit(solution)/shard_map/gather | solution.py:90
  10.8 0.0 copy-done
  10.8 0.7 convolution_convert_fusion
  11.5 0.9 slice_select_fusion.1
  12.4 0.0 copy-start.1
  12.4 0.0 all-reduce.3.cloned.1.call-update
  12.4 0.0 all-gather.2.cloned.1.call-start
  12.5 34.7 %all-reduce.3.cloned.1.call-done = (bf16[128,1280]{1,0:T(8,128)(2,1)}, bf16[128,1280]{1,0:T(8,128)(2,1)}) async-done(((bf16[128,1280]{1,0:T(8,128)(2,1)}, bf16[128,1280]{1,0:T(8,128)(2,1)}), (bf16[128,1280]{1,0:T(8,128)(2,1)}, bf16[128,1280]{1,0:T(8,128)(2,1)})) %all-reduce.3.cloned.1.call-update) | async-done | bytes 655376 | tf_op jit(solution)/shard_map/psum | solution.py:35
  47.2 1.7 %collective-permute-start = (bf16[1,128,1280]{2,1,0:T(8,128)(2,1)}, bf16[1,128,1280]{2,1,0:T(8,128)(2,1)S(1)}, u32[]{:S(2)}, u32[]{:S(2)}) collective-permute-start(bf16[1,128,1280]{2,1,0:T(8,128)(2,1)} %bitcast.90), channel_id=1, source_target_pairs={{0,1},{1,0},{2,3},{3,2},{4,5},{5,4},{6,7},{7,6},{8,9},{9,8},{10,11... | collective-permute-start | bytes 983048 | tf_op jit(solution)/shard_map/ppermute | solution.py:22
  48.8 0.0 all-gather.2.cloned.1.call-update
  48.9 6.1 %collective-permute-done = bf16[1,128,1280]{2,1,0:T(8,128)(2,1)S(1)} collective-permute-done((bf16[1,128,1280]{2,1,0:T(8,128)(2,1)}, bf16[1,128,1280]{2,1,0:T(8,128)(2,1)S(1)}, u32[]{:S(2)}, u32[]{:S(2)}) %collective-permute-start) | collective-permute-done | bytes 327712 | tf_op jit(solution)/shard_map/ppermute | solution.py:22
  55.0 1.0 pad_maximum_fusion.2
  56.0 1.0 fusion.42
  57.0 2.6 %collective-permute-start.1 = (bf16[2,128,1280]{2,1,0:T(8,128)(2,1)}, bf16[2,128,1280]{2,1,0:T(8,128)(2,1)}, u32[]{:S(2)}, u32[]{:S(2)}) collective-permute-start(bf16[2,128,1280]{2,1,0:T(8,128)(2,1)} %get-tuple-element.10), channel_id=1, source_target_pairs={{0,2},{1,3},{2,0},{3,1},{4,6},{5,7},{6,4},{7,5},{8,10},{9,11},{10,... | collective-permute-start | bytes 1966088 | tf_op jit(solution)/shard_map/ppermute | solution.py:22
  59.6 0.0 copy-done.1
  59.6 1.6 %convolution_convert_fusion.1 = bf16[256,640]{1,0:T(8,128)(2,1)S(1)} fusion(bf16[256,640]{1,0:T(8,128)(2,1)S(1)} %bitcast.82, bf16[640,640]{1,0:T(8,128)(2,1)} %param.10), kind=kOutput, calls=%fused_computation.24 | convolution fusion | flops 209879040 | bytes 1474560 | tf_op jit(solution)/shard_map/dot_general | solution.py:86
  61.2 0.9 copy.12
  62.1 47.4 %collective-permute-done.1 = bf16[2,128,1280]{2,1,0:T(8,128)(2,1)} collective-permute-done((bf16[2,128,1280]{2,1,0:T(8,128)(2,1)}, bf16[2,128,1280]{2,1,0:T(8,128)(2,1)}, u32[]{:S(2)}, u32[]{:S(2)}) %collective-permute-start.1) | collective-permute-done | bytes 655392 | tf_op jit(solution)/shard_map/ppermute | solution.py:22
  109.5 1.2 pad_maximum_fusion.1
  110.7 0.2 reverse_select_fusion
  111.0 0.0 all-gather.2.cloned.1.call-done
  111.0 3.0 %fusion.6 = (bf16[1024,640]{1,0:T(8,128)(2,1)}, bf16[1024,640]{1,0:T(8,128)(2,1)}) fusion(bf16[512,1280]{1,0:T(8,128)(2,1)S(1)} %bitcast.80, bf16[512,1280]{1,0:T(8,128)(2,1)} %all-gather.2.cloned.1.call-done), kind=kLoop, calls=%fused_computation.12 | loop fusion | flops 5242880 | bytes 5242880 | tf_op jit(solution)/shard_map/concatenate | solution.py:61
  114.0 1.6 %copy.13 = bf16[1024,640]{0,1:T(8,128)(2,1)S(1)} copy(bf16[1024,640]{1,0:T(8,128)(2,1)} %get-tuple-element.7) | data formatting | bytes 2621440 | tf_op jit(solution)/shard_map/slice | solution.py:62
  115.6 2.5 %copy.14 = bf16[1024,640]{0,1:T(8,128)(2,1)} copy(bf16[1024,640]{1,0:T(8,128)(2,1)} %get-tuple-element.8) | data formatting | bytes 2621440 | tf_op jit(solution)/shard_map/slice | solution.py:63
  118.1 2.6 %multiply_reduce_fusion = (f32[10,256]{1,0:T(8,128)S(1)}, f32[10,256,1024]{2,1,0:T(8,128)S(1)}) fusion(bf16[256,10,64]{0,2,1:T(8,128)(2,1)} %bitcast.84, bf16[1024,10,64]{0,2,1:T(8,128)(2,1)S(1)} %bitcast.78), kind=kOutput, calls=%fused_computation.2 | convolution fusion | flops 340784640 | bytes 12134400 | tf_op jit(solution)/shard_map/qhd,khd->hqk/dot_general | solution.py:64
  120.7 0.0 copy-start.3
  120.7 2.1 %fusion = f32[10,256]{1,0:T(8,128)S(1)} fusion(f32[10,256,1024]{2,1,0:T(8,128)S(1)} %get-tuple-element.28, f32[10,256]{1,0:T(8,128)S(1)} %get-tuple-element.22), kind=kLoop, calls=%fused_computation.3 | loop fusion | flops 7861760 | bytes 10506240 | tf_op jit(solution)/shard_map/reduce_sum | solution.py:70
  122.8 0.0 copy-done.3
  122.8 0.0 copy-start.5
  122.8 0.0 copy-start.6
  122.8 2.3 %fusion.20 = bf16[256,10,64]{0,2,1:T(8,128)(2,1)S(1)} fusion(bf16[1024,10,64]{0,2,1:T(8,128)(2,1)S(1)} %bitcast.87, f32[10,256,1024]{2,1,0:T(8,128)S(1)} %get-tuple-element.28, f32[10,256]{1,0:T(8,128)S(1)} %get-tuple-element.22, f32[256,10]{0,1:T(8,128)S(1)} %bitcast.95, f32[256,10]{0,1:T(8,128)S(1)} %get-tuple-element.21), kind=kOutput, calls=%fused_computation.26 | convolution fusion | flops 343900160 | bytes 12154880 | tf_op jit(solution)/shard_map/hqk,khd->qhd/dot_general | solution.py:71
  125.1 0.0 copy-start.4
  125.1 0.0 copy-done.5
  125.1 0.6 multiply_reduce_fusion.1
  125.7 0.0 copy-done.6
  125.7 0.1 multiply_convert_fusion.1
  125.9 4.4 %collective-permute-start.2 = (bf16[1,128,640]{2,1,0:T(8,128)(2,1)S(1)}, bf16[1,128,640]{2,1,0:T(8,128)(2,1)S(1)}, u32[]{:S(2)}, u32[]{:S(2)}) collective-permute-start(bf16[1,128,640]{2,1,0:T(8,128)(2,1)S(1)} %get-tuple-element.19), channel_id=1, source_target_pairs={{0,4},{4,8},{8,12},{1,5},{5,9},{9,13},{2,6},{6,10},{10,14},{3,7},{... | collective-permute-start | bytes 491528 | tf_op jit(solution)/shard_map/ppermute | solution.py:45
  130.3 1.9 %collective-permute-start.3 = (bf16[1,128,640]{2,1,0:T(8,128)(2,1)S(1)}, bf16[1,128,640]{2,1,0:T(8,128)(2,1)S(1)}, u32[]{:S(2)}, u32[]{:S(2)}) collective-permute-start(bf16[1,128,640]{2,1,0:T(8,128)(2,1)S(1)} %get-tuple-element.20), channel_id=1, source_target_pairs={{4,0},{8,4},{12,8},{5,1},{9,5},{13,9},{6,2},{10,6},{14,10},{7,3},{... | collective-permute-start | bytes 491528 | tf_op jit(solution)/shard_map/ppermute | solution.py:46
  132.2 0.0 copy-done.4
  132.2 0.5 fusion.30
  132.7 0.0 collective-permute-done.2
  132.7 4.2 %collective-permute-done.3 = bf16[1,128,640]{2,1,0:T(8,128)(2,1)S(1)} collective-permute-done((bf16[1,128,640]{2,1,0:T(8,128)(2,1)S(1)}, bf16[1,128,640]{2,1,0:T(8,128)(2,1)S(1)}, u32[]{:S(2)}, u32[]{:S(2)}) %collective-permute-start.3) | collective-permute-done | bytes 163872 | tf_op jit(solution)/shard_map/ppermute | solution.py:46
  136.9 0.1 pad_maximum_fusion.6
  137.0 0.5 fusion.28
  137.4 0.0 copy-start.2
  137.5 0.5 multiply_convert_fusion
  138.0 2.1 %collective-permute-start.4 = (bf16[1,128,640]{2,1,0:T(8,128)(2,1)S(1)}, bf16[1,128,640]{2,1,0:T(8,128)(2,1)S(1)}, u32[]{:S(2)}, u32[]{:S(2)}) collective-permute-start(bf16[1,128,640]{2,1,0:T(8,128)(2,1)S(1)} %get-tuple-element.15), channel_id=1, source_target_pairs={{0,4},{4,8},{8,12},{1,5},{5,9},{9,13},{2,6},{6,10},{10,14},{3,7},{... | collective-permute-start | bytes 491528 | tf_op jit(solution)/shard_map/ppermute | solution.py:45
  140.1 2.4 %collective-permute-start.5 = (bf16[1,128,640]{2,1,0:T(8,128)(2,1)S(1)}, bf16[1,128,640]{2,1,0:T(8,128)(2,1)S(1)}, u32[]{:S(2)}, u32[]{:S(2)}) collective-permute-start(bf16[1,128,640]{2,1,0:T(8,128)(2,1)S(1)} %get-tuple-element.16), channel_id=1, source_target_pairs={{4,0},{8,4},{12,8},{5,1},{9,5},{13,9},{6,2},{10,6},{14,10},{7,3},{... | collective-permute-start | bytes 491528 | tf_op jit(solution)/shard_map/ppermute | solution.py:46
  142.5 0.0 copy-done.2
  142.5 0.5 fusion.25
  143.0 0.0 collective-permute-done.4
  143.0 3.7 %collective-permute-done.5 = bf16[1,128,640]{2,1,0:T(8,128)(2,1)S(1)} collective-permute-done((bf16[1,128,640]{2,1,0:T(8,128)(2,1)S(1)}, bf16[1,128,640]{2,1,0:T(8,128)(2,1)S(1)}, u32[]{:S(2)}, u32[]{:S(2)}) %collective-permute-start.5) | collective-permute-done | bytes 163872 | tf_op jit(solution)/shard_map/ppermute | solution.py:46
  146.7 0.1 pad_maximum_fusion.4
  146.8 0.5 fusion.23
  147.2 1.2 fusion.16
  (5 shorter events, 0.1 us)
Async XLA Ops:
  6.5 4.3 %copy-start = (bf16[640,1280]{1,0:T(8,128)(2,1)S(1)}, bf16[640,1280]{1,0:T(8,128)(2,1)}, u32[]{:S(2)}) copy-start(bf16[640,1280]{1,0:T(8,128)(2,1)} %param.11) | copy-start | bytes 4915204
  6.5 40.6 %all-reduce.3.cloned.1.call-start = ((), (), s32[]{:S(2)}) async-start(), calls=%async_computation.1 | async-start | bytes 1310720 | tf_op jit(solution)/shard_map/psum | solution.py:35
  12.4 47.2 %copy-start.1 = (bf16[2,128,640]{2,1,0:T(8,128)(2,1)S(1)}, bf16[2,128,640]{2,1,0:T(8,128)(2,1)}, u32[]{:S(2)}) copy-start(bf16[2,128,640]{2,1,0:T(8,128)(2,1)} %param.8) | copy-start | bytes 983044
  12.4 98.6 %all-gather.2.cloned.1.call-start = ((), (), s32[]{:S(2)}) async-start(), calls=%async_computation | async-start | bytes 1638400 | tf_op jit(solution)/shard_map/all_gather | solution.py:106
  47.2 7.8 %collective-permute-start = (bf16[1,128,1280]{2,1,0:T(8,128)(2,1)}, bf16[1,128,1280]{2,1,0:T(8,128)(2,1)S(1)}, u32[]{:S(2)}, u32[]{:S(2)}) collective-permute-start(bf16[1,128,1280]{2,1,0:T(8,128)(2,1)} %bitcast.90), channel_id=1, source_target_pairs={{0,1},{1,0},{2,3},{3,2},{4,5},{5,4},{6,7},{7,6},{8,9},{9,8},{10,11... | collective-permute-start | bytes 983048 | tf_op jit(solution)/shard_map/ppermute | solution.py:22
  57.0 52.6 %collective-permute-start.1 = (bf16[2,128,1280]{2,1,0:T(8,128)(2,1)}, bf16[2,128,1280]{2,1,0:T(8,128)(2,1)}, u32[]{:S(2)}, u32[]{:S(2)}) collective-permute-start(bf16[2,128,1280]{2,1,0:T(8,128)(2,1)} %get-tuple-element.10), channel_id=1, source_target_pairs={{0,2},{1,3},{2,0},{3,1},{4,6},{5,7},{6,4},{7,5},{8,10},{9,11},{10,... | collective-permute-start | bytes 1966088 | tf_op jit(solution)/shard_map/ppermute | solution.py:22
  120.7 2.1 %copy-start.3 = (bf16[1024,640]{0,1:T(8,128)(2,1)S(1)}, bf16[1024,640]{0,1:T(8,128)(2,1)}, u32[]{:S(2)}) copy-start(bf16[1024,640]{0,1:T(8,128)(2,1)} %copy.14) | copy-start | bytes 3932164
  122.8 2.4 %copy-start.5 = (bf16[640,640]{1,0:T(8,128)(2,1)S(1)}, bf16[640,640]{1,0:T(8,128)(2,1)}, u32[]{:S(2)}) copy-start(bf16[640,640]{1,0:T(8,128)(2,1)} %param.12) | copy-start | bytes 2457604
  122.8 2.9 %copy-start.6 = (f32[640]{0:T(1024)S(1)}, f32[640]{0:T(1024)}, u32[]{:S(2)}) copy-start(f32[640]{0:T(1024)} %param.13) | copy-start | bytes 7684
  125.1 7.1 %copy-start.4 = (bf16[3,640,640]{2,1,0:T(8,128)(2,1)S(1)}, bf16[3,640,640]{2,1,0:T(8,128)(2,1)}, u32[]{:S(2)}) copy-start(bf16[3,640,640]{2,1,0:T(8,128)(2,1)} %param.14) | copy-start | bytes 7372804
  125.9 6.8 %collective-permute-start.2 = (bf16[1,128,640]{2,1,0:T(8,128)(2,1)S(1)}, bf16[1,128,640]{2,1,0:T(8,128)(2,1)S(1)}, u32[]{:S(2)}, u32[]{:S(2)}) collective-permute-start(bf16[1,128,640]{2,1,0:T(8,128)(2,1)S(1)} %get-tuple-element.19), channel_id=1, source_target_pairs={{0,4},{4,8},{8,12},{1,5},{5,9},{9,13},{2,6},{6,10},{10,14},{3,7},{... | collective-permute-start | bytes 491528 | tf_op jit(solution)/shard_map/ppermute | solution.py:45
  130.3 6.6 %collective-permute-start.3 = (bf16[1,128,640]{2,1,0:T(8,128)(2,1)S(1)}, bf16[1,128,640]{2,1,0:T(8,128)(2,1)S(1)}, u32[]{:S(2)}, u32[]{:S(2)}) collective-permute-start(bf16[1,128,640]{2,1,0:T(8,128)(2,1)S(1)} %get-tuple-element.20), channel_id=1, source_target_pairs={{4,0},{8,4},{12,8},{5,1},{9,5},{13,9},{6,2},{10,6},{14,10},{7,3},{... | collective-permute-start | bytes 491528 | tf_op jit(solution)/shard_map/ppermute | solution.py:46
  137.4 5.1 %copy-start.2 = (bf16[3,640,640]{2,1,0:T(8,128)(2,1)S(1)}, bf16[3,640,640]{2,1,0:T(8,128)(2,1)}, u32[]{:S(2)}) copy-start(bf16[3,640,640]{2,1,0:T(8,128)(2,1)} %param.15) | copy-start | bytes 7372804
  138.0 5.0 %collective-permute-start.4 = (bf16[1,128,640]{2,1,0:T(8,128)(2,1)S(1)}, bf16[1,128,640]{2,1,0:T(8,128)(2,1)S(1)}, u32[]{:S(2)}, u32[]{:S(2)}) collective-permute-start(bf16[1,128,640]{2,1,0:T(8,128)(2,1)S(1)} %get-tuple-element.15), channel_id=1, source_target_pairs={{0,4},{4,8},{8,12},{1,5},{5,9},{9,13},{2,6},{6,10},{10,14},{3,7},{... | collective-permute-start | bytes 491528 | tf_op jit(solution)/shard_map/ppermute | solution.py:45
  140.1 6.6 %collective-permute-start.5 = (bf16[1,128,640]{2,1,0:T(8,128)(2,1)S(1)}, bf16[1,128,640]{2,1,0:T(8,128)(2,1)S(1)}, u32[]{:S(2)}, u32[]{:S(2)}) collective-permute-start(bf16[1,128,640]{2,1,0:T(8,128)(2,1)S(1)} %get-tuple-element.16), channel_id=1, source_target_pairs={{4,0},{8,4},{12,8},{5,1},{9,5},{13,9},{6,2},{10,6},{14,10},{7,3},{... | collective-permute-start | bytes 491528 | tf_op jit(solution)/shard_map/ppermute | solution.py:46
Sparse Core Ops, SparseCore 0:
  12.6 34.5 all-reduce.2
  49.0 58.5 all-gather.1
